TPU v7x, 32 devices: a whole 2x2x4 slice. The times are simulated.
32 devices in a mesh: seq: 8 (over y, x, core), head: 4 (over z).
Axes of the slice: x: 2, y: 2, z: 4, core: 2. Of those that a mesh axis runs over, the one named last changes fastest.
Arguments:
- hidden: bfloat16 [4096, 2048], P(('seq', 'head')), may hold values from -41 to 41
- w_qkv: bfloat16 [2048, 3072], replicated, may hold values from -0.125 to 0.125
- w_out: bfloat16 [2048, 2048], replicated, may hold values from -0.125 to 0.125
- seg_ids: int32 [4096], replicated, may hold values from 0 to 7, never falling along the last dimension, each value on 1 to 2048 neighbouring positions
- live: int32 [4096], replicated, may hold values 0 or 1
- page_table: int32 [256], replicated, may hold values from 0 to 255, as said below
Outputs:
- mixed: bfloat16 [4096, 2048], P(('seq', 'head'))
- kv_pool: bfloat16 [8, 256, 16, 128], P('head', 'seq')
Inputs may be any that keep to these rules, and one draw needn't show every extreme that they name: `page_table`: A permutation of the 256 pages; pool shard r along seq holds pages r * 32 to (r + 1) * 32 - 1, and the 32 logical pages of each seq group go exactly 4 to each pool shard.
All inputs are finite; a program needn't handle non-finite values.
Results may differ from a plain program's by a relative error of at most 0.0059.
The roundings to bfloat16 on the way count: a program that leaves them out, or rounds other values in their place, can miss the bound.
Values may be sent and summed in bfloat16 or wider, within the bound.
No kernel may reach another device: no remote copies, remote signals or barrier semaphores. Data moves between devices by JAX's collectives and lax.ppermute only.
A program may use at most 128 MiB of HBM per device.

v0:
```python
import functools

import jax
import jax.numpy as jnp
from jax import lax
from jax.experimental import pallas as pl
from jax.experimental.pallas import tpu as pltpu
from jax.sharding import PartitionSpec as P

KVH = 8
HD = 64
PAGE = 16
QPK = 4
TQ = 256
BK = 512
INTERPRET = False


def attention_kernel(seg_sm, base_sm, q_ref, kv_ref, qseg_ref, qidx_ref, kseg_ref,
                     o_ref, m_sc, l_sc, acc_sc):
    qi = pl.program_id(0)
    ki = pl.program_id(1)
    groups = q_ref.shape[0]
    tq = q_ref.shape[1] // QPK
    bk = kv_ref.shape[1]

    @pl.when(ki == 0)
    def _():
        m_sc[...] = jnp.full(m_sc.shape, -1e30, jnp.float32)
        l_sc[...] = jnp.zeros(l_sc.shape, jnp.float32)
        acc_sc[...] = jnp.zeros(acc_sc.shape, jnp.float32)

    q_first = base_sm[0] + qi * tq
    q_last = q_first + tq - 1
    k_first = ki * bk
    k_last = k_first + bk - 1
    active = (k_first <= q_last) & (seg_sm[k_first] <= seg_sm[q_last]) & (seg_sm[k_last] >= seg_sm[q_first])

    @pl.when(active)
    def _():
        kidx = k_first + lax.broadcasted_iota(jnp.int32, (1, bk), 1)
        qidx = qidx_ref[...]
        allowed = ((kseg_ref[...] == qseg_ref[...]) & (kidx <= qidx)) | (kidx == qidx)
        for g in range(groups):
            scores = lax.dot_general(
                q_ref[g], kv_ref[g], (((1,), (1,)), ((), ())), preferred_element_type=jnp.float32
            ) * 0.015625
            masked = jnp.where(allowed, scores, -1e30)
            m_old = m_sc[g]
            m_new = jnp.maximum(m_old, jnp.max(masked, axis=1, keepdims=True))
            m_row = jnp.where(m_new == -1e30, 0.0, m_new)
            weights = jnp.exp(masked - m_row)
            factor = jnp.exp(m_old - m_new)
            l_sc[g] = l_sc[g] * factor + jnp.sum(weights, axis=1, keepdims=True)
            update = jnp.dot(weights.astype(jnp.bfloat16), kv_ref[g], preferred_element_type=jnp.float32)
            acc_sc[g] = acc_sc[g] * factor + update
            m_sc[g] = m_new

    @pl.when(ki == pl.num_programs(1) - 1)
    def _():
        for g in range(groups):
            for c in range(QPK):
                lo = (g * QPK + c) * HD
                part = acc_sc[g, c * tq:(c + 1) * tq, HD:] / l_sc[g, c * tq:(c + 1) * tq]
                o_ref[:, lo:lo + HD] = part.astype(o_ref.dtype)


def attend(queries, keyvals_all, seg_ids, live, first_row):
    group_rows, groups = queries.shape[:2]
    tokens = keyvals_all.shape[1]
    tq = min(TQ, group_rows)
    nq = group_rows // tq
    bk = min(BK, tokens)
    nk = tokens // bk
    rows = QPK * tq
    q = queries.reshape(nq, tq, groups, QPK, HD).transpose(0, 2, 3, 1, 4).reshape(nq, groups, rows, HD)
    q = jnp.concatenate([q, jnp.zeros_like(q)], axis=-1)
    tok = first_row + jnp.arange(group_rows, dtype=jnp.int32)
    seg_here = lax.dynamic_slice_in_dim(seg_ids, first_row, group_rows, 0)

    def column(x):
        return jnp.broadcast_to(x.reshape(nq, 1, tq), (nq, QPK, tq)).reshape(nq, rows, 1)

    qidx = column(tok)
    qseg = column(seg_here)
    kseg = jnp.where(live == 1, seg_ids, -1).reshape(1, tokens)
    base = jnp.reshape(first_row, (1,)).astype(jnp.int32)

    def kmap(qi, ki, seg_sm, base_sm):
        return jnp.minimum(ki, (base_sm[0] + qi * tq + tq - 1) // bk)

    grid_spec = pltpu.PrefetchScalarGridSpec(
        num_scalar_prefetch=2,
        grid=(nq, nk),
        in_specs=[
            pl.BlockSpec((None, groups, rows, 2 * HD), lambda qi, ki, s, b: (qi, 0, 0, 0)),
            pl.BlockSpec((groups, bk, 2 * HD), lambda qi, ki, s, b: (0, kmap(qi, ki, s, b), 0)),
            pl.BlockSpec((None, rows, 1), lambda qi, ki, s, b: (qi, 0, 0)),
            pl.BlockSpec((None, rows, 1), lambda qi, ki, s, b: (qi, 0, 0)),
            pl.BlockSpec((1, bk), lambda qi, ki, s, b: (0, kmap(qi, ki, s, b))),
        ],
        out_specs=pl.BlockSpec((tq, groups * QPK * HD), lambda qi, ki, s, b: (qi, 0)),
        scratch_shapes=[
            pltpu.VMEM((groups, rows, 1), jnp.float32),
            pltpu.VMEM((groups, rows, 1), jnp.float32),
            pltpu.VMEM((groups, rows, 2 * HD), jnp.float32),
        ],
    )
    return pl.pallas_call(
        attention_kernel,
        out_shape=jax.ShapeDtypeStruct((group_rows, groups * QPK * HD), jnp.bfloat16),
        grid_spec=grid_spec,
        compiler_params=pltpu.CompilerParams(dimension_semantics=("arbitrary", "arbitrary")),
        interpret=INTERPRET,
    )(seg_ids, base, q, keyvals_all, qseg, qidx, kseg)


def exchange(chunks, heads_n, head_at):
    got = [lax.dynamic_index_in_dim(chunks, head_at, 0, keepdims=False)]
    for d in range(1, heads_n):
        mine = lax.dynamic_index_in_dim(chunks, (head_at + d) % heads_n, 0, keepdims=False)
        pairs = [(i, (i + d) % heads_n) for i in range(heads_n)]
        got.append(lax.ppermute(mine, "head", pairs))
    return got


def shards(hidden, w_qkv, w_out, seg_ids, live, page_table):
    heads_n = lax.axis_size("head")
    head_at = lax.axis_index("head")
    seq_at = lax.axis_index("seq")
    groups_here = KVH // heads_n
    per_group = (QPK + 2) * HD
    columns = groups_here * per_group
    local = jnp.dot(hidden, w_qkv, preferred_element_type=jnp.float32).astype(jnp.bfloat16)
    own_rows = local.shape[0]
    local = local.reshape(own_rows, heads_n, groups_here, QPK + 2, HD)
    kv_local = local[:, :, :, QPK:].reshape(own_rows, heads_n, groups_here, 2 * HD).transpose(1, 2, 0, 3)
    kv_got = exchange(kv_local, heads_n, head_at)
    kv_by_shift = jnp.stack(kv_got, axis=0)
    shift_of = (head_at - jnp.arange(heads_n, dtype=jnp.int32)) % heads_n
    kv_by_src = jnp.take(kv_by_shift, shift_of, axis=0)
    group_rows = own_rows * heads_n
    keyvals = kv_by_src.transpose(1, 0, 2, 3).reshape(groups_here, group_rows, 2 * HD)
    piece = lax.all_gather(keyvals, "seq", axis=1, tiled=True)
    q_local = local[:, :, :, :QPK].reshape(own_rows, heads_n, groups_here * QPK * HD).transpose(1, 0, 2)
    q_by_shift = jnp.stack(exchange(q_local, heads_n, head_at), axis=0)
    q_by_src = jnp.take(q_by_shift, shift_of, axis=0)
    queries = q_by_src.reshape(group_rows, groups_here, QPK, HD)
    first_row = (seq_at * group_rows).astype(jnp.int32)
    attended = attend(queries, piece, seg_ids, live, first_row)
    width = attended.shape[1]
    att_got = exchange(attended.reshape(heads_n, own_rows, width), heads_n, head_at)
    total = None
    for d in range(heads_n):
        src_head = (head_at - d) % heads_n
        w_rows = lax.dynamic_slice_in_dim(w_out, src_head * width, width, 0)
        partial = jnp.dot(att_got[d], w_rows, preferred_element_type=jnp.float32)
        total = partial if total is None else total + partial
    mixed = total.astype(jnp.bfloat16)
    pages_n = page_table.shape[0]
    page_count = pages_n // lax.axis_size("seq")
    all_pages = piece.reshape(groups_here, pages_n, PAGE, 2 * HD)
    wanted = seq_at * page_count + jnp.arange(page_count, dtype=jnp.int32)
    hits = page_table[None, :] == wanted[:, None]
    logical = jnp.sum(jnp.where(hits, jnp.arange(pages_n, dtype=jnp.int32)[None, :], 0), axis=1)
    kv_pool = jnp.take(all_pages, logical, axis=1)
    return (mixed, kv_pool)


def solution(mesh):
    placed = (P(("seq", "head"), None), P(), P(), P(), P(), P())
    return jax.shard_map(
        shards,
        mesh=mesh,
        in_specs=placed,
        out_specs=(P(("seq", "head"), None), P("head", "seq", None, None)),
        check_vma=False,
    )
```

profile of v0, /device:TPU:5, one launch (start us, length us, event | category | flops | bytes accessed | tf_op | source)
XLA Modules:
  0.0 110.1 jit_solution(5260931766133378718)
XLA Ops:
  7.3 0.9 copy-done
  8.2 6.4 %convolution_convert_fusion = bf16[128,3072]{1,0:T(8,128)(2,1)S(1)} fusion(bf16[128,2048]{1,0:T(8,128)(2,1)S(1)} %copy-done, bf16[2048,3072]{1,0:T(8,128)(2,1)} %param.7), kind=kOutput, calls=%fused_computation.3 | convolution fusion | flops 1611005952 | bytes 13893632 | tf_op jit(solution)/shard_map/dot_general | solution.py:134
  15.2 1.3 %collective-permute-start.3 = (bf16[2,128,128]{2,1,0:T(8,128)(2,1)S(1)}, bf16[2,128,128]{2,1,0:T(8,128)(2,1)S(1)}, u32[]{:S(2)}, u32[]{:S(2)}) collective-permute-start(bf16[2,128,128]{2,1,0:T(8,128)(2,1)S(1)} %bitcast.80), channel_id=1, source_target_pairs={{0,1},{1,2},{2,3},{3,0},{4,5},{5,6},{6,7},{7,4},{8,9},{9,10},{10,1... | collective-permute-start | bytes 196616 | tf_op jit(solution)/shard_map/ppermute | solution.py:123
  16.7 2.4 %collective-permute-start.4 = (bf16[2,128,128]{2,1,0:T(8,128)(2,1)S(1)}, bf16[2,128,128]{2,1,0:T(8,128)(2,1)S(1)}, u32[]{:S(2)}, u32[]{:S(2)}) collective-permute-start(bf16[2,128,128]{2,1,0:T(8,128)(2,1)S(1)} %bitcast.81), channel_id=1, source_target_pairs={{0,2},{1,3},{2,0},{3,1},{4,6},{5,7},{6,4},{7,5},{8,10},{9,11},{10,... | collective-permute-start | bytes 196616 | tf_op jit(solution)/shard_map/ppermute | solution.py:123
  19.2 1.1 %collective-permute-start.5 = (bf16[2,128,128]{2,1,0:T(8,128)(2,1)S(1)}, bf16[2,128,128]{2,1,0:T(8,128)(2,1)S(1)}, u32[]{:S(2)}, u32[]{:S(2)}) collective-permute-start(bf16[2,128,128]{2,1,0:T(8,128)(2,1)S(1)} %bitcast.82), channel_id=1, source_target_pairs={{0,3},{1,0},{2,1},{3,2},{4,7},{5,4},{6,5},{7,6},{8,11},{9,8},{10,9... | collective-permute-start | bytes 196616 | tf_op jit(solution)/shard_map/ppermute | solution.py:123
  20.5 2.7 %collective-permute-done.4 = bf16[2,128,128]{2,1,0:T(8,128)(2,1)S(1)} collective-permute-done((bf16[2,128,128]{2,1,0:T(8,128)(2,1)S(1)}, bf16[2,128,128]{2,1,0:T(8,128)(2,1)S(1)}, u32[]{:S(2)}, u32[]{:S(2)}) %collective-permute-start.4) | collective-permute-done | bytes 65568 | tf_op jit(solution)/shard_map/ppermute | solution.py:123
  24.1 0.7 copy.37
  25.1 2.0 %collective-permute-start = (bf16[128,512]{1,0:T(8,128)(2,1)S(1)}, bf16[128,512]{1,0:T(8,128)(2,1)S(1)}, u32[]{:S(2)}, u32[]{:S(2)}) collective-permute-start(bf16[128,512]{1,0:T(8,128)(2,1)S(1)} %bitcast.73), channel_id=1, source_target_pairs={{0,1},{1,2},{2,3},{3,0},{4,5},{5,6},{6,7},{7,4},{8,9},{9,10},{10,1... | collective-permute-start | bytes 393224 | tf_op jit(solution)/shard_map/ppermute | solution.py:123
  27.2 0.7 collective-permute-start.1
  28.1 1.5 %collective-permute-start.2 = (bf16[128,512]{1,0:T(8,128)(2,1)S(1)}, bf16[128,512]{1,0:T(8,128)(2,1)S(1)}, u32[]{:S(2)}, u32[]{:S(2)}) collective-permute-start(bf16[128,512]{1,0:T(8,128)(2,1)S(1)} %bitcast.75), channel_id=1, source_target_pairs={{0,3},{1,0},{2,1},{3,2},{4,7},{5,4},{6,5},{7,6},{8,11},{9,8},{10,9... | collective-permute-start | bytes 393224 | tf_op jit(solution)/shard_map/ppermute | solution.py:123
  30.7 1.9 %reshape.172.qseg_ref = s32[2,1024,1]{2,1,0:T(8,128)} reshape(s32[2,4,256]{2,1,0:T(4,128)S(1)} %broadcast_in_dim.73) | data formatting | bytes 16384 | tf_op jit(solution)/shard_map/reshape | solution.py:82
  32.7 1.9 %reshape.173.qidx_ref = s32[2,1024,1]{2,1,0:T(8,128)} reshape(s32[2,4,256]{2,1,0:T(4,128)S(1)} %broadcast_in_dim.74) | data formatting | bytes 16384 | tf_op jit(solution)/shard_map/reshape | solution.py:82
  34.5 3.4 %collective-permute-done.1 = bf16[128,512]{1,0:T(8,128)(2,1)S(1)} collective-permute-done((bf16[128,512]{1,0:T(8,128)(2,1)S(1)}, bf16[128,512]{1,0:T(8,128)(2,1)S(1)}, u32[]{:S(2)}, u32[]{:S(2)}) %collective-permute-start.1) | collective-permute-done | bytes 131104 | tf_op jit(solution)/shard_map/ppermute | solution.py:123
  40.4 1.2 %concatenate.3.q_ref = bf16[2,2,1024,128]{3,2,1,0:T(8,128)(2,1)} pad(bf16[2,2,1024,64]{3,2,1,0:T(8,128)(2,1)S(1)} %bitcast.62, bf16[]{:T(256)} %constant.154.clone.1), padding=0_0x0_0x0_0x0_64 | pad | bytes 1572866 | tf_op jit(solution)/shard_map/concatenate | solution.py:77
  41.6 13.0 %all-gather.2.cloned.1.call-done.kv_ref = bf16[2,4096,128]{2,1,0:T(8,128)(2,1)} async-done(((bf16[2,512,128]{2,1,0:T(8,128)(2,1)}), bf16[2,4096,128]{2,1,0:T(8,128)(2,1)}) %all-gather.2.cloned.1.call-update) | async-done | bytes 2097168 | tf_op jit(solution)/shard_map/all_gather | solution.py:144
  54.6 31.8 %shard_map.77 = bf16[512,512]{1,0:T(8,128)(2,1)} custom-call(s32[4096]{0:T(1024)} %seg_sm.1, s32[1]{0:T(128)} %bitcast.base_sm, bf16[2,2,1024,128]{3,2,1,0:T(8,128)(2,1)} %concatenate.3.q_ref, bf16[2,4096,128]{2,1,0:T(8,128)(2,1)} %all-gather.2.cloned.1.call-done.kv_ref, s32[2,1024,1]{2,1,0:T(8,128)} %reshape.172.qseg_ref, s32[2,1024,1]{2,1,0:T(8,128)} %reshape.173.qidx_ref, ...), custom_call_target="tpu_custom_call" | custom-call | tf_op jit(solution)/shard_map/pallas_call | solution.py:109
  86.3 1.1 dynamic-slice_bitcast_fusion.1
  87.4 1.3 %collective-permute-start.6 = (bf16[128,512]{1,0:T(8,128)(2,1)S(1)}, bf16[128,512]{1,0:T(8,128)(2,1)S(1)}, u32[]{:S(2)}, u32[]{:S(2)}) collective-permute-start(bf16[128,512]{1,0:T(8,128)(2,1)S(1)} %get-tuple-element.8), channel_id=1, source_target_pairs={{0,1},{1,2},{2,3},{3,0},{4,5},{5,6},{6,7},{7,4},{8,9},{9,10},{10,1... | collective-permute-start | bytes 393224 | tf_op jit(solution)/shard_map/ppermute | solution.py:123
  88.7 2.1 %collective-permute-start.8 = (bf16[128,512]{1,0:T(8,128)(2,1)S(1)}, bf16[128,512]{1,0:T(8,128)(2,1)S(1)}, u32[]{:S(2)}, u32[]{:S(2)}) collective-permute-start(bf16[128,512]{1,0:T(8,128)(2,1)S(1)} %get-tuple-element.7), channel_id=1, source_target_pairs={{0,3},{1,0},{2,1},{3,2},{4,7},{5,4},{6,5},{7,6},{8,11},{9,8},{10,9... | collective-permute-start | bytes 393224 | tf_op jit(solution)/shard_map/ppermute | solution.py:123
  91.0 2.2 %gather_fusion.2 = bf16[32,2,16,128]{3,2,1,0:T(8,128)(2,1)S(1)} fusion(bf16[2,256,16,128]{3,2,1,0:T(8,128)(2,1)} %bitcast.65, s32[1024]{0:T(1024)S(1)} %pad_clamp_fusion), kind=kCustom, calls=%fused_computation.2 | custom fusion | bytes 524416 | tf_op jit(solution)/shard_map/jit(_take)/gather | solution.py:166
  94.1 2.1 %fusion.6 = f32[128,2048]{1,0:T(8,128)S(1)} fusion(bf16[2048,2048]{1,0:T(8,128)(2,1)} %param.8, s32[]{:T(128)S(6)} %select_n.181, bf16[4,128,512]{2,1,0:T(8,128)(2,1)} %bitcast.67, s32[]{:T(128)S(6)} %select_n.164), kind=kOutput, calls=%fused_computation.12 | convolution fusion | flops 268435456 | bytes 3276808 | tf_op jit(solution)/shard_map/dot_general | solution.py:157
  96.2 2.1 %convolution_add_fusion.1 = f32[128,2048]{1,0:T(8,128)S(1)} fusion(f32[128,2048]{1,0:T(8,128)S(1)} %fusion.6, bf16[128,512]{1,0:T(8,128)(2,1)S(1)} %collective-permute-done.6, bf16[2048,2048]{1,0:T(8,128)(2,1)} %param.8, s32[]{:T(128)S(6)} %select_n.183), kind=kOutput, calls=%fused_computation.6 | convolution fusion | flops 268697600 | bytes 4325380 | tf_op jit(solution)/shard_map/dot_general | solution.py:157
  98.3 2.0 %fusion.2 = f32[128,2048]{1,0:T(8,128)S(1)} fusion(bf16[128,512]{1,0:T(8,128)(2,1)S(1)} %collective-permute-done.8, bf16[2048,2048]{1,0:T(8,128)(2,1)} %param.8, s32[]{:T(128)S(6)} %select_n.187), kind=kOutput, calls=%fused_computation.8 | convolution fusion | flops 268435456 | bytes 3276804 | tf_op jit(solution)/shard_map/dot_general | solution.py:157
  100.4 2.9 %fusion.1 = bf16[128,2048]{1,0:T(8,128)(2,1)} fusion(f32[128,2048]{1,0:T(8,128)S(1)} %fusion.2, f32[128,2048]{1,0:T(8,128)S(1)} %convolution_add_fusion.1, bf16[128,512]{1,0:T(8,128)(2,1)S(1)} %collective-permute-done.7, bf16[2048,2048]{1,0:T(8,128)(2,1)} %param.8, s32[]{:T(128)S(6)} %select_n.185), kind=kOutput, calls=%fused_computation.7 | convolution fusion | flops 269221888 | bytes 4849668 | tf_op jit(solution)/shard_map/dot_general | solution.py:157
  (58 shorter events, 7.1 us)
Async XLA Ops:
  7.2 1.0 copy-start
  7.2 47.4 %all-gather.2.cloned.1.call-start = ((), (), s32[]{:S(2)}) async-start(), calls=%async_computation | async-start | bytes 2359296 | tf_op jit(solution)/shard_map/all_gather | solution.py:144
  14.6 15.0 %copy-start.3 = (s32[256]{0:T(256)S(1)}, s32[256]{0:T(256)}, u32[]{:S(2)}) copy-start(s32[256]{0:T(256)} %param.11) | copy-start | bytes 3076
  14.6 15.3 %copy-start.1 = (s32[4096]{0:T(1024)S(1)}, s32[4096]{0:T(1024)}, u32[]{:S(2)}) copy-start(s32[4096]{0:T(1024)} %seg_sm.1) | copy-start | bytes 49156
  14.6 15.3 %copy-start.2 = (s32[4096]{0:T(1024)S(1)}, s32[4096]{0:T(1024)}, u32[]{:S(2)}) copy-start(s32[4096]{0:T(1024)} %param.10) | copy-start | bytes 49156
  15.2 5.3 %collective-permute-start.3 = (bf16[2,128,128]{2,1,0:T(8,128)(2,1)S(1)}, bf16[2,128,128]{2,1,0:T(8,128)(2,1)S(1)}, u32[]{:S(2)}, u32[]{:S(2)}) collective-permute-start(bf16[2,128,128]{2,1,0:T(8,128)(2,1)S(1)} %bitcast.80), channel_id=1, source_target_pairs={{0,1},{1,2},{2,3},{3,0},{4,5},{5,6},{6,7},{7,4},{8,9},{9,10},{10,1... | collective-permute-start | bytes 196616 | tf_op jit(solution)/shard_map/ppermute | solution.py:123
  16.7 6.5 %collective-permute-start.4 = (bf16[2,128,128]{2,1,0:T(8,128)(2,1)S(1)}, bf16[2,128,128]{2,1,0:T(8,128)(2,1)S(1)}, u32[]{:S(2)}, u32[]{:S(2)}) collective-permute-start(bf16[2,128,128]{2,1,0:T(8,128)(2,1)S(1)} %bitcast.81), channel_id=1, source_target_pairs={{0,2},{1,3},{2,0},{3,1},{4,6},{5,7},{6,4},{7,5},{8,10},{9,11},{10,... | collective-permute-start | bytes 196616 | tf_op jit(solution)/shard_map/ppermute | solution.py:123
  19.2 4.2 %collective-permute-start.5 = (bf16[2,128,128]{2,1,0:T(8,128)(2,1)S(1)}, bf16[2,128,128]{2,1,0:T(8,128)(2,1)S(1)}, u32[]{:S(2)}, u32[]{:S(2)}) collective-permute-start(bf16[2,128,128]{2,1,0:T(8,128)(2,1)S(1)} %bitcast.82), channel_id=1, source_target_pairs={{0,3},{1,0},{2,1},{3,2},{4,7},{5,4},{6,5},{7,6},{8,11},{9,8},{10,9... | collective-permute-start | bytes 196616 | tf_op jit(solution)/shard_map/ppermute | solution.py:123
  25.1 9.4 %collective-permute-start = (bf16[128,512]{1,0:T(8,128)(2,1)S(1)}, bf16[128,512]{1,0:T(8,128)(2,1)S(1)}, u32[]{:S(2)}, u32[]{:S(2)}) collective-permute-start(bf16[128,512]{1,0:T(8,128)(2,1)S(1)} %bitcast.73), channel_id=1, source_target_pairs={{0,1},{1,2},{2,3},{3,0},{4,5},{5,6},{6,7},{7,4},{8,9},{9,10},{10,1... | collective-permute-start | bytes 393224 | tf_op jit(solution)/shard_map/ppermute | solution.py:123
  27.2 10.7 %collective-permute-start.1 = (bf16[128,512]{1,0:T(8,128)(2,1)S(1)}, bf16[128,512]{1,0:T(8,128)(2,1)S(1)}, u32[]{:S(2)}, u32[]{:S(2)}) collective-permute-start(bf16[128,512]{1,0:T(8,128)(2,1)S(1)} %bitcast.74), channel_id=1, source_target_pairs={{0,2},{1,3},{2,0},{3,1},{4,6},{5,7},{6,4},{7,5},{8,10},{9,11},{10,... | collective-permute-start | bytes 393224 | tf_op jit(solution)/shard_map/ppermute | solution.py:123
  28.1 9.9 %collective-permute-start.2 = (bf16[128,512]{1,0:T(8,128)(2,1)S(1)}, bf16[128,512]{1,0:T(8,128)(2,1)S(1)}, u32[]{:S(2)}, u32[]{:S(2)}) collective-permute-start(bf16[128,512]{1,0:T(8,128)(2,1)S(1)} %bitcast.75), channel_id=1, source_target_pairs={{0,3},{1,0},{2,1},{3,2},{4,7},{5,4},{6,5},{7,6},{8,11},{9,8},{10,9... | collective-permute-start | bytes 393224 | tf_op jit(solution)/shard_map/ppermute | solution.py:123
  87.4 8.8 %collective-permute-start.6 = (bf16[128,512]{1,0:T(8,128)(2,1)S(1)}, bf16[128,512]{1,0:T(8,128)(2,1)S(1)}, u32[]{:S(2)}, u32[]{:S(2)}) collective-permute-start(bf16[128,512]{1,0:T(8,128)(2,1)S(1)} %get-tuple-element.8), channel_id=1, source_target_pairs={{0,1},{1,2},{2,3},{3,0},{4,5},{5,6},{6,7},{7,4},{8,9},{9,10},{10,1... | collective-permute-start | bytes 393224 | tf_op jit(solution)/shard_map/ppermute | solution.py:123
  88.7 9.6 %collective-permute-start.8 = (bf16[128,512]{1,0:T(8,128)(2,1)S(1)}, bf16[128,512]{1,0:T(8,128)(2,1)S(1)}, u32[]{:S(2)}, u32[]{:S(2)}) collective-permute-start(bf16[128,512]{1,0:T(8,128)(2,1)S(1)} %get-tuple-element.7), channel_id=1, source_target_pairs={{0,3},{1,0},{2,1},{3,2},{4,7},{5,4},{6,5},{7,6},{8,11},{9,8},{10,9... | collective-permute-start | bytes 393224 | tf_op jit(solution)/shard_map/ppermute | solution.py:123
  90.7 9.6 %collective-permute-start.7 = (bf16[128,512]{1,0:T(8,128)(2,1)S(1)}, bf16[128,512]{1,0:T(8,128)(2,1)S(1)}, u32[]{:S(2)}, u32[]{:S(2)}) collective-permute-start(bf16[128,512]{1,0:T(8,128)(2,1)S(1)} %get-tuple-element.6), channel_id=1, source_target_pairs={{0,2},{1,3},{2,0},{3,1},{4,6},{5,7},{6,4},{7,5},{8,10},{9,11},{10,... | collective-permute-start | bytes 393224 | tf_op jit(solution)/shard_map/ppermute | solution.py:123
Sparse Core Ops, SparseCore 0:
  25.0 29.5 all-gather.1
where the time goes:
time: 110 us
  Pallas kernels  31.8 us (29%)
  waiting for transfers between devices  19.3 us (18%)
  matrix products  15.5 us (14%)
  local copies, waits for them, and re-layouts  14.7 us (13%)
  between operations  14.4 us (13%)
  starting transfers between devices  12.8 us (12%)
  other arithmetic  1.62 us (1%)
    pallas_call x1, Pallas kernels, attend(): pl.pallas_call(attention_kernel, out_shape=jax.ShapeDtypeStruct((group_ro...  31.8 us
    all_gather x1, waiting for transfers between devices, shards(): piece = lax.all_gather(keyvals, 'seq', axis=1, tiled=True)  13 us
    ppermute x9, starting transfers between devices, exchange(): got.append(lax.ppermute(mine, 'head', pairs))  12.7 us
    dot_general x4, matrix products, shards(): partial = jnp.dot(att_got[d], w_rows, preferred_element_type=jnp.float32)  9.12 us
    dot_general x1, matrix products, shards(): jnp.dot(hidden, w_qkv, preferred_element_type=jnp.float32)  6.37 us
    ppermute x9, waiting for transfers between devices, exchange(): got.append(lax.ppermute(mine, 'head', pairs))  6.34 us
    reshape x2, local copies, waits for them, and re-layouts, column(): jnp.broadcast_to(x.reshape(nq, 1, tq), (nq, QPK, tq)).reshape(nq, rows, 1)  3.77 us
    unnamed x15, local copies, waits for them, and re-layouts  2.25 us
  transfers between devices with their start and end apart: 10, of which 4 were waited for; matrix products, arithmetic and copies ran while one was open for 17% of the time, Pallas kernels for 0%

commit v1 on v0

--- a/solution.py
+++ b/solution.py
@@ -11,7 +11,7 @@
 HD = 64
 PAGE = 16
 QPK = 4
-TQ = 256
+TQ = 512
 BK = 512
 INTERPRET = False
 

time: 110 us -> 113 us (1.027)
  the two profiles are of different devices: /device:TPU:5 before, /device:TPU:7 now
where the time goes in v1:
time: 113 us; the launch traced here: 112 us
  Pallas kernels  34.7 us (31%)
  waiting for transfers between devices  20 us (18%)
  matrix products  15.5 us (14%)
  local copies, waits for them, and re-layouts  14.4 us (13%)
  between operations  14.4 us (13%)
  starting transfers between devices  12.1 us (11%)
  other arithmetic  1.19 us (1%)
    pallas_call x1, Pallas kernels, attend(): pl.pallas_call(attention_kernel, out_shape=jax.ShapeDtypeStruct((group_ro...  34.7 us
    ppermute x9, starting transfers between devices, exchange(): got.append(lax.ppermute(mine, 'head', pairs))  12 us
    all_gather x1, waiting for transfers between devices, shards(): piece = lax.all_gather(keyvals, 'seq', axis=1, tiled=True)  10.7 us
    ppermute x9, waiting for transfers between devices, exchange(): got.append(lax.ppermute(mine, 'head', pairs))  9.24 us
    dot_general x4, matrix products, shards(): partial = jnp.dot(att_got[d], w_rows, preferred_element_type=jnp.float32)  9.12 us
    dot_general x1, matrix products, shards(): jnp.dot(hidden, w_qkv, preferred_element_type=jnp.float32)  6.37 us
    broadcast_in_dim x4, local copies, waits for them, and re-layouts, column(): jnp.broadcast_to(x.reshape(nq, 1, tq), (nq, QPK, tq)).reshape(nq, rows, 1)  3.78 us
  transfers between devices with their start and end apart: 10, of which 4 were waited for; matrix products, arithmetic and copies ran while one was open for 16% of the time, Pallas kernels for 0%

profile of v1, /device:TPU:7, one launch (start us, length us, event | category | flops | bytes accessed | tf_op | source)
XLA Modules:
  0.0 112.2 jit_solution(13211200043208115385)
XLA Ops:
  7.3 0.9 copy-done
  8.2 6.4 %convolution_convert_fusion = bf16[128,3072]{1,0:T(8,128)(2,1)S(1)} fusion(bf16[128,2048]{1,0:T(8,128)(2,1)S(1)} %copy-done, bf16[2048,3072]{1,0:T(8,128)(2,1)} %param.7), kind=kOutput, calls=%fused_computation.3 | convolution fusion | flops 1611005952 | bytes 13893632 | tf_op jit(solution)/shard_map/dot_general | solution.py:134
  15.2 1.4 %collective-permute-start.3 = (bf16[2,128,128]{2,1,0:T(8,128)(2,1)S(1)}, bf16[2,128,128]{2,1,0:T(8,128)(2,1)S(1)}, u32[]{:S(2)}, u32[]{:S(2)}) collective-permute-start(bf16[2,128,128]{2,1,0:T(8,128)(2,1)S(1)} %bitcast.77), channel_id=1, source_target_pairs={{0,1},{1,2},{2,3},{3,0},{4,5},{5,6},{6,7},{7,4},{8,9},{9,10},{10,1... | collective-permute-start | bytes 196616 | tf_op jit(solution)/shard_map/ppermute | solution.py:123
  16.7 2.4 %collective-permute-start.4 = (bf16[2,128,128]{2,1,0:T(8,128)(2,1)S(1)}, bf16[2,128,128]{2,1,0:T(8,128)(2,1)S(1)}, u32[]{:S(2)}, u32[]{:S(2)}) collective-permute-start(bf16[2,128,128]{2,1,0:T(8,128)(2,1)S(1)} %bitcast.78), channel_id=1, source_target_pairs={{0,2},{1,3},{2,0},{3,1},{4,6},{5,7},{6,4},{7,5},{8,10},{9,11},{10,... | collective-permute-start | bytes 196616 | tf_op jit(solution)/shard_map/ppermute | solution.py:123
  19.2 1.1 collective-permute-start.5
  20.5 2.7 %collective-permute-done.4 = bf16[2,128,128]{2,1,0:T(8,128)(2,1)S(1)} collective-permute-done((bf16[2,128,128]{2,1,0:T(8,128)(2,1)S(1)}, bf16[2,128,128]{2,1,0:T(8,128)(2,1)S(1)}, u32[]{:S(2)}, u32[]{:S(2)}) %collective-permute-start.4) | collective-permute-done | bytes 65568 | tf_op jit(solution)/shard_map/ppermute | solution.py:123
  24.1 0.7 copy.37
  25.1 2.4 %collective-permute-start.2 = (bf16[128,512]{1,0:T(8,128)(2,1)S(1)}, bf16[128,512]{1,0:T(8,128)(2,1)S(1)}, u32[]{:S(2)}, u32[]{:S(2)}) collective-permute-start(bf16[128,512]{1,0:T(8,128)(2,1)S(1)} %bitcast.70), channel_id=1, source_target_pairs={{0,3},{1,0},{2,1},{3,2},{4,7},{5,4},{6,5},{7,6},{8,11},{9,8},{10,9... | collective-permute-start | bytes 393224 | tf_op jit(solution)/shard_map/ppermute | solution.py:123
  28.0 0.9 collective-permute-start.1
  30.0 1.9 %broadcast_in_dim.83.qseg_ref = s32[1,2048,1]{2,1,0:T(8,128)} reshape(s32[4,512]{1,0:T(4,128)S(1)} %broadcast_in_dim.74) | data formatting | bytes 16384 | tf_op jit(solution)/shard_map/broadcast_in_dim | solution.py:82
  31.9 1.9 %broadcast_in_dim.84.qidx_ref = s32[1,2048,1]{2,1,0:T(8,128)} reshape(s32[4,512]{1,0:T(4,128)S(1)} %broadcast_in_dim.76) | data formatting | bytes 16384 | tf_op jit(solution)/shard_map/broadcast_in_dim | solution.py:82
  33.8 6.3 %collective-permute-done.1 = bf16[128,512]{1,0:T(8,128)(2,1)S(1)} collective-permute-done((bf16[128,512]{1,0:T(8,128)(2,1)S(1)}, bf16[128,512]{1,0:T(8,128)(2,1)S(1)}, u32[]{:S(2)}, u32[]{:S(2)}) %collective-permute-start.1) | collective-permute-done | bytes 131104 | tf_op jit(solution)/shard_map/ppermute | solution.py:123
  41.8 1.2 %concatenate.3.q_ref = bf16[1,2,2048,128]{3,2,1,0:T(8,128)(2,1)} pad(bf16[1,2,2048,64]{3,2,1,0:T(8,128)(2,1)S(1)} %bitcast.59, bf16[]{:T(256)} %constant.150.clone.1), padding=0_0x0_0x0_0x0_64 | pad | bytes 1572866 | tf_op jit(solution)/shard_map/concatenate | solution.py:77
  43.0 10.7 %all-gather.2.cloned.1.call-done.kv_ref = bf16[2,4096,128]{2,1,0:T(8,128)(2,1)} async-done(((bf16[2,512,128]{2,1,0:T(8,128)(2,1)}), bf16[2,4096,128]{2,1,0:T(8,128)(2,1)}) %all-gather.2.cloned.1.call-update) | async-done | bytes 2097168 | tf_op jit(solution)/shard_map/all_gather | solution.py:144
  53.7 34.7 %shard_map.77 = bf16[512,512]{1,0:T(8,128)(2,1)} custom-call(s32[4096]{0:T(1024)} %seg_sm.1, s32[1]{0:T(128)} %bitcast.base_sm, bf16[1,2,2048,128]{3,2,1,0:T(8,128)(2,1)} %concatenate.3.q_ref, bf16[2,4096,128]{2,1,0:T(8,128)(2,1)} %all-gather.2.cloned.1.call-done.kv_ref, s32[1,2048,1]{2,1,0:T(8,128)} %broadcast_in_dim.83.qseg_ref, ...), custom_call_target="tpu_custom_call" | custom-call | tf_op jit(solution)/shard_map/pallas_call | solution.py:109
  88.4 1.1 dynamic-slice_bitcast_fusion.1
  89.5 1.2 %collective-permute-start.6 = (bf16[128,512]{1,0:T(8,128)(2,1)S(1)}, bf16[128,512]{1,0:T(8,128)(2,1)S(1)}, u32[]{:S(2)}, u32[]{:S(2)}) collective-permute-start(bf16[128,512]{1,0:T(8,128)(2,1)S(1)} %get-tuple-element.8), channel_id=1, source_target_pairs={{0,1},{1,2},{2,3},{3,0},{4,5},{5,6},{6,7},{7,4},{8,9},{9,10},{10,1... | collective-permute-start | bytes 393224 | tf_op jit(solution)/shard_map/ppermute | solution.py:123
  90.8 2.1 %collective-permute-start.8 = (bf16[128,512]{1,0:T(8,128)(2,1)S(1)}, bf16[128,512]{1,0:T(8,128)(2,1)S(1)}, u32[]{:S(2)}, u32[]{:S(2)}) collective-permute-start(bf16[128,512]{1,0:T(8,128)(2,1)S(1)} %get-tuple-element.7), channel_id=1, source_target_pairs={{0,3},{1,0},{2,1},{3,2},{4,7},{5,4},{6,5},{7,6},{8,11},{9,8},{10,9... | collective-permute-start | bytes 393224 | tf_op jit(solution)/shard_map/ppermute | solution.py:123
  93.2 2.2 %gather_fusion.2 = bf16[32,2,16,128]{3,2,1,0:T(8,128)(2,1)S(1)} fusion(bf16[2,256,16,128]{3,2,1,0:T(8,128)(2,1)} %bitcast.62, s32[1024]{0:T(1024)S(1)} %pad_clamp_fusion), kind=kCustom, calls=%fused_computation.2 | custom fusion | bytes 524416 | tf_op jit(solution)/shard_map/jit(_take)/gather | solution.py:166
  95.5 0.7 copy.40
  96.2 2.1 %fusion.6 = f32[128,2048]{1,0:T(8,128)S(1)} fusion(bf16[2048,2048]{1,0:T(8,128)(2,1)} %param.8, s32[]{:T(128)S(6)} %select_n.179, bf16[4,128,512]{2,1,0:T(8,128)(2,1)} %bitcast.64, s32[]{:T(128)S(6)} %select_n.164), kind=kOutput, calls=%fused_computation.12 | convolution fusion | flops 268435456 | bytes 3276808 | tf_op jit(solution)/shard_map/dot_general | solution.py:157
  98.3 2.1 %convolution_add_fusion.1 = f32[128,2048]{1,0:T(8,128)S(1)} fusion(f32[128,2048]{1,0:T(8,128)S(1)} %fusion.6, bf16[128,512]{1,0:T(8,128)(2,1)S(1)} %collective-permute-done.6, bf16[2048,2048]{1,0:T(8,128)(2,1)} %param.8, s32[]{:T(128)S(6)} %select_n.181), kind=kOutput, calls=%fused_computation.6 | convolution fusion | flops 268697600 | bytes 4325380 | tf_op jit(solution)/shard_map/dot_general | solution.py:157
  100.4 2.0 %fusion.2 = f32[128,2048]{1,0:T(8,128)S(1)} fusion(bf16[128,512]{1,0:T(8,128)(2,1)S(1)} %collective-permute-done.8, bf16[2048,2048]{1,0:T(8,128)(2,1)} %param.8, s32[]{:T(128)S(6)} %select_n.185), kind=kOutput, calls=%fused_computation.8 | convolution fusion | flops 268435456 | bytes 3276804 | tf_op jit(solution)/shard_map/dot_general | solution.py:157
  102.5 2.9 %fusion.1 = bf16[128,2048]{1,0:T(8,128)(2,1)} fusion(f32[128,2048]{1,0:T(8,128)S(1)} %fusion.2, f32[128,2048]{1,0:T(8,128)S(1)} %convolution_add_fusion.1, bf16[128,512]{1,0:T(8,128)(2,1)S(1)} %collective-permute-done.7, bf16[2048,2048]{1,0:T(8,128)(2,1)} %param.8, s32[]{:T(128)S(6)} %select_n.183), kind=kOutput, calls=%fused_computation.7 | convolution fusion | flops 269221888 | bytes 4849668 | tf_op jit(solution)/shard_map/dot_general | solution.py:157
  (55 shorter events, 5.8 us)
Async XLA Ops:
  7.2 1.0 copy-start
  7.2 46.5 %all-gather.2.cloned.1.call-start = ((), (), s32[]{:S(2)}) async-start(), calls=%async_computation | async-start | bytes 2359296 | tf_op jit(solution)/shard_map/all_gather | solution.py:144
  14.6 14.3 %copy-start.3 = (s32[256]{0:T(256)S(1)}, s32[256]{0:T(256)}, u32[]{:S(2)}) copy-start(s32[256]{0:T(256)} %param.11) | copy-start | bytes 3076
  14.6 14.5 %copy-start.1 = (s32[4096]{0:T(1024)S(1)}, s32[4096]{0:T(1024)}, u32[]{:S(2)}) copy-start(s32[4096]{0:T(1024)} %seg_sm.1) | copy-start | bytes 49156
  14.6 14.5 %copy-start.2 = (s32[4096]{0:T(1024)S(1)}, s32[4096]{0:T(1024)}, u32[]{:S(2)}) copy-start(s32[4096]{0:T(1024)} %param.10) | copy-start | bytes 49156
  15.2 5.3 %collective-permute-start.3 = (bf16[2,128,128]{2,1,0:T(8,128)(2,1)S(1)}, bf16[2,128,128]{2,1,0:T(8,128)(2,1)S(1)}, u32[]{:S(2)}, u32[]{:S(2)}) collective-permute-start(bf16[2,128,128]{2,1,0:T(8,128)(2,1)S(1)} %bitcast.77), channel_id=1, source_target_pairs={{0,1},{1,2},{2,3},{3,0},{4,5},{5,6},{6,7},{7,4},{8,9},{9,10},{10,1... | collective-permute-start | bytes 196616 | tf_op jit(solution)/shard_map/ppermute | solution.py:123
  16.7 6.5 %collective-permute-start.4 = (bf16[2,128,128]{2,1,0:T(8,128)(2,1)S(1)}, bf16[2,128,128]{2,1,0:T(8,128)(2,1)S(1)}, u32[]{:S(2)}, u32[]{:S(2)}) collective-permute-start(bf16[2,128,128]{2,1,0:T(8,128)(2,1)S(1)} %bitcast.78), channel_id=1, source_target_pairs={{0,2},{1,3},{2,0},{3,1},{4,6},{5,7},{6,4},{7,5},{8,10},{9,11},{10,... | collective-permute-start | bytes 196616 | tf_op jit(solution)/shard_map/ppermute | solution.py:123
  19.2 4.2 %collective-permute-start.5 = (bf16[2,128,128]{2,1,0:T(8,128)(2,1)S(1)}, bf16[2,128,128]{2,1,0:T(8,128)(2,1)S(1)}, u32[]{:S(2)}, u32[]{:S(2)}) collective-permute-start(bf16[2,128,128]{2,1,0:T(8,128)(2,1)S(1)} %bitcast.79), channel_id=1, source_target_pairs={{0,3},{1,0},{2,1},{3,2},{4,7},{5,4},{6,5},{7,6},{8,11},{9,8},{10,9... | collective-permute-start | bytes 196616 | tf_op jit(solution)/shard_map/ppermute | solution.py:123
  25.1 8.7 %collective-permute-start.2 = (bf16[128,512]{1,0:T(8,128)(2,1)S(1)}, bf16[128,512]{1,0:T(8,128)(2,1)S(1)}, u32[]{:S(2)}, u32[]{:S(2)}) collective-permute-start(bf16[128,512]{1,0:T(8,128)(2,1)S(1)} %bitcast.70), channel_id=1, source_target_pairs={{0,3},{1,0},{2,1},{3,2},{4,7},{5,4},{6,5},{7,6},{8,11},{9,8},{10,9... | collective-permute-start | bytes 393224 | tf_op jit(solution)/shard_map/ppermute | solution.py:123
  27.6 6.1 %collective-permute-start = (bf16[128,512]{1,0:T(8,128)(2,1)S(1)}, bf16[128,512]{1,0:T(8,128)(2,1)S(1)}, u32[]{:S(2)}, u32[]{:S(2)}) collective-permute-start(bf16[128,512]{1,0:T(8,128)(2,1)S(1)} %bitcast.71), channel_id=1, source_target_pairs={{0,1},{1,2},{2,3},{3,0},{4,5},{5,6},{6,7},{7,4},{8,9},{9,10},{10,1... | collective-permute-start | bytes 393224 | tf_op jit(solution)/shard_map/ppermute | solution.py:123
  28.0 12.1 %collective-permute-start.1 = (bf16[128,512]{1,0:T(8,128)(2,1)S(1)}, bf16[128,512]{1,0:T(8,128)(2,1)S(1)}, u32[]{:S(2)}, u32[]{:S(2)}) collective-permute-start(bf16[128,512]{1,0:T(8,128)(2,1)S(1)} %bitcast.72), channel_id=1, source_target_pairs={{0,2},{1,3},{2,0},{3,1},{4,6},{5,7},{6,4},{7,5},{8,10},{9,11},{10,... | collective-permute-start | bytes 393224 | tf_op jit(solution)/shard_map/ppermute | solution.py:123
  89.5 8.8 %collective-permute-start.6 = (bf16[128,512]{1,0:T(8,128)(2,1)S(1)}, bf16[128,512]{1,0:T(8,128)(2,1)S(1)}, u32[]{:S(2)}, u32[]{:S(2)}) collective-permute-start(bf16[128,512]{1,0:T(8,128)(2,1)S(1)} %get-tuple-element.8), channel_id=1, source_target_pairs={{0,1},{1,2},{2,3},{3,0},{4,5},{5,6},{6,7},{7,4},{8,9},{9,10},{10,1... | collective-permute-start | bytes 393224 | tf_op jit(solution)/shard_map/ppermute | solution.py:123
  90.8 9.7 %collective-permute-start.8 = (bf16[128,512]{1,0:T(8,128)(2,1)S(1)}, bf16[128,512]{1,0:T(8,128)(2,1)S(1)}, u32[]{:S(2)}, u32[]{:S(2)}) collective-permute-start(bf16[128,512]{1,0:T(8,128)(2,1)S(1)} %get-tuple-element.7), channel_id=1, source_target_pairs={{0,3},{1,0},{2,1},{3,2},{4,7},{5,4},{6,5},{7,6},{8,11},{9,8},{10,9... | collective-permute-start | bytes 393224 | tf_op jit(solution)/shard_map/ppermute | solution.py:123
  92.8 9.6 %collective-permute-start.7 = (bf16[128,512]{1,0:T(8,128)(2,1)S(1)}, bf16[128,512]{1,0:T(8,128)(2,1)S(1)}, u32[]{:S(2)}, u32[]{:S(2)}) collective-permute-start(bf16[128,512]{1,0:T(8,128)(2,1)S(1)} %get-tuple-element.6), channel_id=1, source_target_pairs={{0,2},{1,3},{2,0},{3,1},{4,6},{5,7},{6,4},{7,5},{8,10},{9,11},{10,... | collective-permute-start | bytes 393224 | tf_op jit(solution)/shard_map/ppermute | solution.py:123
Sparse Core Ops, SparseCore 0:
  25.0 28.6 all-gather.1

commit v2 on v1

--- a/solution.py
+++ b/solution.py
@@ -141,13 +141,16 @@
     kv_by_src = jnp.take(kv_by_shift, shift_of, axis=0)
     group_rows = own_rows * heads_n
     keyvals = kv_by_src.transpose(1, 0, 2, 3).reshape(groups_here, group_rows, 2 * HD)
-    piece = lax.all_gather(keyvals, "seq", axis=1, tiled=True)
+    pieces = [lax.all_gather(keyvals[g:g + 1], "seq", axis=1, tiled=True) for g in range(groups_here)]
+    piece = jnp.concatenate(pieces, axis=0)
     q_local = local[:, :, :, :QPK].reshape(own_rows, heads_n, groups_here * QPK * HD).transpose(1, 0, 2)
     q_by_shift = jnp.stack(exchange(q_local, heads_n, head_at), axis=0)
     q_by_src = jnp.take(q_by_shift, shift_of, axis=0)
     queries = q_by_src.reshape(group_rows, groups_here, QPK, HD)
     first_row = (seq_at * group_rows).astype(jnp.int32)
-    attended = attend(queries, piece, seg_ids, live, first_row)
+    attended = jnp.concatenate(
+        [attend(queries[:, g:g + 1], pieces[g], seg_ids, live, first_row) for g in range(groups_here)], axis=1
+    )
     width = attended.shape[1]
     att_got = exchange(attended.reshape(heads_n, own_rows, width), heads_n, head_at)
     total = None

time: 113 us -> 125 us (1.11)
  the two profiles are of different devices: /device:TPU:7 before, /device:TPU:13 now
where the time goes in v2:
time: 125 us; the launch traced here: 124 us
  Pallas kernels  42.1 us (34%)
  waiting for transfers between devices  19.8 us (16%)
  matrix products  15.4 us (12%)
  local copies, waits for them, and re-layouts  14.8 us (12%)
  between operations  14.5 us (12%)
  starting transfers between devices  14.1 us (11%)
  other arithmetic  3.69 us (3%)
    pallas_call x2, Pallas kernels, attend(): pl.pallas_call(attention_kernel, out_shape=jax.ShapeDtypeStruct((group_ro...  42.1 us
    ppermute x9, starting transfers between devices, exchange(): got.append(lax.ppermute(mine, 'head', pairs))  14 us
    all_gather x2, waiting for transfers between devices, shards(): lax.all_gather(keyvals[g:g + 1], 'seq', axis=1, tiled=True)  12.2 us
    dot_general x4, matrix products, shards(): partial = jnp.dot(att_got[d], w_rows, preferred_element_type=jnp.float32)  9.04 us
    ppermute x9, waiting for transfers between devices, exchange(): got.append(lax.ppermute(mine, 'head', pairs))  7.58 us
    dot_general x1, matrix products, shards(): jnp.dot(hidden, w_qkv, preferred_element_type=jnp.float32)  6.37 us
    broadcast_in_dim x4, local copies, waits for them, and re-layouts, column(): jnp.broadcast_to(x.reshape(nq, 1, tq), (nq, QPK, tq)).reshape(nq, rows, 1)  3.75 us
  transfers between devices with their start and end apart: 11, of which 5 were waited for; matrix products, arithmetic and copies ran while one was open for 16% of the time, Pallas kernels for 17%

profile of v2, /device:TPU:13, one launch (start us, length us, event | category | flops | bytes accessed | tf_op | source)
XLA Modules:
  0.0 124.4 jit_solution(9125194012830663774)
XLA Ops:
  7.3 0.9 copy-done
  8.2 6.4 %convolution_convert_fusion = bf16[128,3072]{1,0:T(8,128)(2,1)S(1)} fusion(bf16[128,2048]{1,0:T(8,128)(2,1)S(1)} %copy-done, bf16[2048,3072]{1,0:T(8,128)(2,1)} %param.7), kind=kOutput, calls=%fused_computation.3 | convolution fusion | flops 1611005952 | bytes 13893632 | tf_op jit(solution)/shard_map/dot_general | solution.py:134
  15.5 2.4 %collective-permute-start.4 = (bf16[2,128,128]{2,1,0:T(8,128)(2,1)S(1)}, bf16[2,128,128]{2,1,0:T(8,128)(2,1)S(1)}, u32[]{:S(2)}, u32[]{:S(2)}) collective-permute-start(bf16[2,128,128]{2,1,0:T(8,128)(2,1)S(1)} %bitcast.89), channel_id=1, source_target_pairs={{0,2},{1,3},{2,0},{3,1},{4,6},{5,7},{6,4},{7,5},{8,10},{9,11},{10,... | collective-permute-start | bytes 196616 | tf_op jit(solution)/shard_map/ppermute | solution.py:123
  18.0 2.2 %collective-permute-start.3 = (bf16[2,128,128]{2,1,0:T(8,128)(2,1)S(1)}, bf16[2,128,128]{2,1,0:T(8,128)(2,1)S(1)}, u32[]{:S(2)}, u32[]{:S(2)}) collective-permute-start(bf16[2,128,128]{2,1,0:T(8,128)(2,1)S(1)} %bitcast.90), channel_id=1, source_target_pairs={{0,1},{1,2},{2,3},{3,0},{4,5},{5,6},{6,7},{7,4},{8,9},{9,10},{10,1... | collective-permute-start | bytes 196616 | tf_op jit(solution)/shard_map/ppermute | solution.py:123
  20.5 2.9 %collective-permute-done.3 = bf16[2,128,128]{2,1,0:T(8,128)(2,1)S(1)} collective-permute-done((bf16[2,128,128]{2,1,0:T(8,128)(2,1)S(1)}, bf16[2,128,128]{2,1,0:T(8,128)(2,1)S(1)}, u32[]{:S(2)}, u32[]{:S(2)}) %collective-permute-start.3) | collective-permute-done | bytes 65568 | tf_op jit(solution)/shard_map/ppermute | solution.py:123
  26.1 2.7 %collective-permute-start.1 = (bf16[128,512]{1,0:T(8,128)(2,1)S(1)}, bf16[128,512]{1,0:T(8,128)(2,1)S(1)}, u32[]{:S(2)}, u32[]{:S(2)}) collective-permute-start(bf16[128,512]{1,0:T(8,128)(2,1)S(1)} %bitcast.83), channel_id=1, source_target_pairs={{0,2},{1,3},{2,0},{3,1},{4,6},{5,7},{6,4},{7,5},{8,10},{9,11},{10,... | collective-permute-start | bytes 393224 | tf_op jit(solution)/shard_map/ppermute | solution.py:123
  30.3 1.9 %broadcast_in_dim.89.qseg_ref = s32[1,2048,1]{2,1,0:T(8,128)} reshape(s32[4,512]{1,0:T(4,128)S(1)} %broadcast_in_dim.80) | data formatting | bytes 16384 | tf_op jit(solution)/shard_map/broadcast_in_dim | solution.py:82
  32.2 1.9 %broadcast_in_dim.90.qidx_ref = s32[1,2048,1]{2,1,0:T(8,128)} reshape(s32[4,512]{1,0:T(4,128)S(1)} %broadcast_in_dim.82) | data formatting | bytes 16384 | tf_op jit(solution)/shard_map/broadcast_in_dim | solution.py:82
  34.1 1.8 %collective-permute-done.1 = bf16[128,512]{1,0:T(8,128)(2,1)S(1)} collective-permute-done((bf16[128,512]{1,0:T(8,128)(2,1)S(1)}, bf16[128,512]{1,0:T(8,128)(2,1)S(1)}, u32[]{:S(2)}, u32[]{:S(2)}) %collective-permute-start.1) | collective-permute-done | bytes 131104 | tf_op jit(solution)/shard_map/ppermute | solution.py:123
  35.9 2.8 %collective-permute-done = bf16[128,512]{1,0:T(8,128)(2,1)S(1)} collective-permute-done((bf16[128,512]{1,0:T(8,128)(2,1)S(1)}, bf16[128,512]{1,0:T(8,128)(2,1)S(1)}, u32[]{:S(2)}, u32[]{:S(2)}) %collective-permute-start) | collective-permute-done | bytes 131104 | tf_op jit(solution)/shard_map/ppermute | solution.py:123
  41.5 0.9 concatenate.12.q_ref
  42.4 7.9 %all-gather.5.cloned.1.call-done.kv_ref = bf16[1,4096,128]{2,1,0:T(8,128)(2,1)} async-done(((bf16[1,512,128]{2,1,0:T(8,128)(2,1)}), bf16[1,4096,128]{2,1,0:T(8,128)(2,1)}) %all-gather.5.cloned.1.call-update) | async-done | bytes 1048592 | tf_op jit(solution)/shard_map/all_gather | solution.py:144
  50.3 21.0 %shard_map.78 = bf16[512,256]{1,0:T(8,128)(2,1)} custom-call(s32[4096]{0:T(1024)} %seg_sm.3, s32[1]{0:T(128)} %bitcast.base_sm, bf16[1,1,2048,128]{3,2,1,0:T(8,128)(2,1)} %concatenate.13.q_ref, bf16[1,4096,128]{2,1,0:T(8,128)(2,1)} %all-gather.5.cloned.1.call-done.kv_ref, s32[1,2048,1]{2,1,0:T(8,128)} %broadcast_in_dim.89.qseg_ref, ...), custom_call_target="tpu_custom_call" | custom-call | tf_op jit(solution)/shard_map/pallas_call | solution.py:109
  71.3 4.3 %all-gather.3.cloned.1.call-done.kv_ref = bf16[1,4096,128]{2,1,0:T(8,128)(2,1)} async-done(((bf16[1,512,128]{2,1,0:T(8,128)(2,1)}), bf16[1,4096,128]{2,1,0:T(8,128)(2,1)}) %all-gather.3.cloned.1.call-update) | async-done | bytes 1048592 | tf_op jit(solution)/shard_map/all_gather | solution.py:144
  75.6 21.1 %shard_map.77 = bf16[512,256]{1,0:T(8,128)(2,1)} custom-call(s32[4096]{0:T(1024)} %seg_sm.3, s32[1]{0:T(128)} %bitcast.base_sm, bf16[1,1,2048,128]{3,2,1,0:T(8,128)(2,1)} %concatenate.12.q_ref, bf16[1,4096,128]{2,1,0:T(8,128)(2,1)} %all-gather.3.cloned.1.call-done.kv_ref, s32[1,2048,1]{2,1,0:T(8,128)} %broadcast_in_dim.89.qseg_ref, ...), custom_call_target="tpu_custom_call" | custom-call | tf_op jit(solution)/shard_map/pallas_call | solution.py:109
  96.7 1.0 pad_maximum_fusion.2
  98.7 1.2 collective-permute-start.6
  99.9 3.9 %collective-permute-start.7 = (bf16[128,512]{1,0:T(8,128)(2,1)}, bf16[128,512]{1,0:T(8,128)(2,1)S(1)}, u32[]{:S(2)}, u32[]{:S(2)}) collective-permute-start(bf16[128,512]{1,0:T(8,128)(2,1)} %get-tuple-element.6), channel_id=1, source_target_pairs={{0,2},{1,3},{2,0},{3,1},{4,6},{5,7},{6,4},{7,5},{8,10},{9,11},{10,... | collective-permute-start | bytes 393224 | tf_op jit(solution)/shard_map/ppermute | solution.py:123
  103.9 1.5 %pad_maximum_fusion = bf16[2,4096,128]{2,1,0:T(8,128)(2,1)} fusion(bf16[1,4096,128]{2,1,0:T(8,128)(2,1)S(1)} %copy-done.1, bf16[1,4096,128]{2,1,0:T(8,128)(2,1)S(1)} %copy-done.2), kind=kLoop, calls=%fused_computation.8 | loop fusion | flops 1048576 | bytes 4194304 | tf_op jit(solution)/shard_map/concatenate | solution.py:145
  105.4 2.2 %gather_fusion.2 = bf16[32,2,16,128]{3,2,1,0:T(8,128)(2,1)S(1)} fusion(bf16[2,256,16,128]{3,2,1,0:T(8,128)(2,1)} %bitcast.69, s32[1024]{0:T(1024)S(1)} %pad_clamp_fusion), kind=kCustom, calls=%fused_computation.2 | custom fusion | bytes 524416 | tf_op jit(solution)/shard_map/jit(_take)/gather | solution.py:169
  108.4 2.0 %fusion.6 = f32[128,2048]{1,0:T(8,128)S(1)} fusion(bf16[2048,2048]{1,0:T(8,128)(2,1)} %param.8, s32[]{:T(128)S(6)} %select_n.175, bf16[4,128,512]{2,1,0:T(8,128)(2,1)S(1)} %bitcast.71, s32[]{:T(128)S(6)} %select_n.160), kind=kOutput, calls=%fused_computation.13 | convolution fusion | flops 268435456 | bytes 3276808 | tf_op jit(solution)/shard_map/dot_general | solution.py:160
  110.5 2.1 %convolution_add_fusion.1 = f32[128,2048]{1,0:T(8,128)S(1)} fusion(f32[128,2048]{1,0:T(8,128)S(1)} %fusion.6, bf16[128,512]{1,0:T(8,128)(2,1)S(1)} %collective-permute-done.6, bf16[2048,2048]{1,0:T(8,128)(2,1)} %param.8, s32[]{:T(128)S(6)} %select_n.177), kind=kOutput, calls=%fused_computation.6 | convolution fusion | flops 268697600 | bytes 4325380 | tf_op jit(solution)/shard_map/dot_general | solution.py:160
  112.6 2.0 %fusion.2 = f32[128,2048]{1,0:T(8,128)S(1)} fusion(bf16[128,512]{1,0:T(8,128)(2,1)S(1)} %collective-permute-done.8, bf16[2048,2048]{1,0:T(8,128)(2,1)} %param.8, s32[]{:T(128)S(6)} %select_n.181), kind=kOutput, calls=%fused_computation.9 | convolution fusion | flops 268435456 | bytes 3276804 | tf_op jit(solution)/shard_map/dot_general | solution.py:160
  114.6 2.9 %fusion.1 = bf16[128,2048]{1,0:T(8,128)(2,1)} fusion(f32[128,2048]{1,0:T(8,128)S(1)} %fusion.2, f32[128,2048]{1,0:T(8,128)S(1)} %convolution_add_fusion.1, bf16[128,512]{1,0:T(8,128)(2,1)S(1)} %collective-permute-done.7, bf16[2048,2048]{1,0:T(8,128)(2,1)} %param.8, s32[]{:T(128)S(6)} %select_n.179), kind=kOutput, calls=%fused_computation.7 | convolution fusion | flops 269221888 | bytes 4849668 | tf_op jit(solution)/shard_map/dot_general | solution.py:160
  (70 shorter events, 9.8 us)
Async XLA Ops:
  7.2 1.0 copy-start
  7.2 43.1 %all-gather.5.cloned.1.call-start = ((), (), s32[]{:S(2)}) async-start(), calls=%async_computation.1 | async-start | bytes 1179648 | tf_op jit(solution)/shard_map/all_gather | solution.py:144
  15.2 5.3 %collective-permute-start.5 = (bf16[2,128,128]{2,1,0:T(8,128)(2,1)S(1)}, bf16[2,128,128]{2,1,0:T(8,128)(2,1)S(1)}, u32[]{:S(2)}, u32[]{:S(2)}) collective-permute-start(bf16[2,128,128]{2,1,0:T(8,128)(2,1)S(1)} %bitcast.88), channel_id=1, source_target_pairs={{0,3},{1,0},{2,1},{3,2},{4,7},{5,4},{6,5},{7,6},{8,11},{9,8},{10,9... | collective-permute-start | bytes 196616 | tf_op jit(solution)/shard_map/ppermute | solution.py:123
  15.5 4.9 %collective-permute-start.4 = (bf16[2,128,128]{2,1,0:T(8,128)(2,1)S(1)}, bf16[2,128,128]{2,1,0:T(8,128)(2,1)S(1)}, u32[]{:S(2)}, u32[]{:S(2)}) collective-permute-start(bf16[2,128,128]{2,1,0:T(8,128)(2,1)S(1)} %bitcast.89), channel_id=1, source_target_pairs={{0,2},{1,3},{2,0},{3,1},{4,6},{5,7},{6,4},{7,5},{8,10},{9,11},{10,... | collective-permute-start | bytes 196616 | tf_op jit(solution)/shard_map/ppermute | solution.py:123
  18.0 5.4 %collective-permute-start.3 = (bf16[2,128,128]{2,1,0:T(8,128)(2,1)S(1)}, bf16[2,128,128]{2,1,0:T(8,128)(2,1)S(1)}, u32[]{:S(2)}, u32[]{:S(2)}) collective-permute-start(bf16[2,128,128]{2,1,0:T(8,128)(2,1)S(1)} %bitcast.90), channel_id=1, source_target_pairs={{0,1},{1,2},{2,3},{3,0},{4,5},{5,6},{6,7},{7,4},{8,9},{9,10},{10,1... | collective-permute-start | bytes 196616 | tf_op jit(solution)/shard_map/ppermute | solution.py:123
  24.0 5.2 %copy-start.6 = (s32[256]{0:T(256)S(1)}, s32[256]{0:T(256)}, u32[]{:S(2)}) copy-start(s32[256]{0:T(256)} %param.11) | copy-start | bytes 3076
  24.0 5.4 %copy-start.4 = (s32[4096]{0:T(1024)S(1)}, s32[4096]{0:T(1024)}, u32[]{:S(2)}) copy-start(s32[4096]{0:T(1024)} %seg_sm.3) | copy-start | bytes 49156
  24.1 5.4 %copy-start.5 = (s32[4096]{0:T(1024)S(1)}, s32[4096]{0:T(1024)}, u32[]{:S(2)}) copy-start(s32[4096]{0:T(1024)} %param.10) | copy-start | bytes 49156
  24.9 50.7 %all-gather.3.cloned.1.call-start = ((), (), s32[]{:S(2)}) async-start(), calls=%async_computation | async-start | bytes 1179648 | tf_op jit(solution)/shard_map/all_gather | solution.py:144
  25.2 8.9 %collective-permute-start.2 = (bf16[128,512]{1,0:T(8,128)(2,1)S(1)}, bf16[128,512]{1,0:T(8,128)(2,1)S(1)}, u32[]{:S(2)}, u32[]{:S(2)}) collective-permute-start(bf16[128,512]{1,0:T(8,128)(2,1)S(1)} %bitcast.82), channel_id=1, source_target_pairs={{0,3},{1,0},{2,1},{3,2},{4,7},{5,4},{6,5},{7,6},{8,11},{9,8},{10,9... | collective-permute-start | bytes 393224 | tf_op jit(solution)/shard_map/ppermute | solution.py:123
  26.1 9.8 %collective-permute-start.1 = (bf16[128,512]{1,0:T(8,128)(2,1)S(1)}, bf16[128,512]{1,0:T(8,128)(2,1)S(1)}, u32[]{:S(2)}, u32[]{:S(2)}) collective-permute-start(bf16[128,512]{1,0:T(8,128)(2,1)S(1)} %bitcast.83), channel_id=1, source_target_pairs={{0,2},{1,3},{2,0},{3,1},{4,6},{5,7},{6,4},{7,5},{8,10},{9,11},{10,... | collective-permute-start | bytes 393224 | tf_op jit(solution)/shard_map/ppermute | solution.py:123
  28.9 9.8 %collective-permute-start = (bf16[128,512]{1,0:T(8,128)(2,1)S(1)}, bf16[128,512]{1,0:T(8,128)(2,1)S(1)}, u32[]{:S(2)}, u32[]{:S(2)}) collective-permute-start(bf16[128,512]{1,0:T(8,128)(2,1)S(1)} %bitcast.84), channel_id=1, source_target_pairs={{0,1},{1,2},{2,3},{3,0},{4,5},{5,6},{6,7},{7,4},{8,9},{9,10},{10,1... | collective-permute-start | bytes 393224 | tf_op jit(solution)/shard_map/ppermute | solution.py:123
  71.3 25.4 %copy-start.3 = (bf16[512,256]{1,0:T(8,128)(2,1)S(1)}, bf16[512,256]{1,0:T(8,128)(2,1)}, u32[]{:S(2)}) copy-start(bf16[512,256]{1,0:T(8,128)(2,1)} %shard_map.78) | copy-start | bytes 786436
  71.3 32.6 %copy-start.1 = (bf16[1,4096,128]{2,1,0:T(8,128)(2,1)S(1)}, bf16[1,4096,128]{2,1,0:T(8,128)(2,1)}, u32[]{:S(2)}) copy-start(bf16[1,4096,128]{2,1,0:T(8,128)(2,1)} %all-gather.5.cloned.1.call-done.kv_ref) | copy-start | bytes 3145732
  75.6 28.3 %copy-start.2 = (bf16[1,4096,128]{2,1,0:T(8,128)(2,1)S(1)}, bf16[1,4096,128]{2,1,0:T(8,128)(2,1)}, u32[]{:S(2)}) copy-start(bf16[1,4096,128]{2,1,0:T(8,128)(2,1)} %all-gather.3.cloned.1.call-done.kv_ref) | copy-start | bytes 3145732
  98.5 14.1 %collective-permute-start.8 = (bf16[128,512]{1,0:T(8,128)(2,1)}, bf16[128,512]{1,0:T(8,128)(2,1)S(1)}, u32[]{:S(2)}, u32[]{:S(2)}) collective-permute-start(bf16[128,512]{1,0:T(8,128)(2,1)} %get-tuple-element.7), channel_id=1, source_target_pairs={{0,3},{1,0},{2,1},{3,2},{4,7},{5,4},{6,5},{7,6},{8,11},{9,8},{10,9... | collective-permute-start | bytes 393224 | tf_op jit(solution)/shard_map/ppermute | solution.py:123
  98.7 11.7 %collective-permute-start.6 = (bf16[128,512]{1,0:T(8,128)(2,1)}, bf16[128,512]{1,0:T(8,128)(2,1)S(1)}, u32[]{:S(2)}, u32[]{:S(2)}) collective-permute-start(bf16[128,512]{1,0:T(8,128)(2,1)} %get-tuple-element.8), channel_id=1, source_target_pairs={{0,1},{1,2},{2,3},{3,0},{4,5},{5,6},{6,7},{7,4},{8,9},{9,10},{10,1... | collective-permute-start | bytes 393224 | tf_op jit(solution)/shard_map/ppermute | solution.py:123
  99.9 14.7 %collective-permute-start.7 = (bf16[128,512]{1,0:T(8,128)(2,1)}, bf16[128,512]{1,0:T(8,128)(2,1)S(1)}, u32[]{:S(2)}, u32[]{:S(2)}) collective-permute-start(bf16[128,512]{1,0:T(8,128)(2,1)} %get-tuple-element.6), channel_id=1, source_target_pairs={{0,2},{1,3},{2,0},{3,1},{4,6},{5,7},{6,4},{7,5},{8,10},{9,11},{10,... | collective-permute-start | bytes 393224 | tf_op jit(solution)/shard_map/ppermute | solution.py:123
Sparse Core Ops, SparseCore 0:
  25.0 25.2 all-gather.4
  52.2 23.3 all-gather.2
